TPU v7x, 512 devices: a whole 4x4x16 slice. The times are simulated.
512 devices in a mesh: expert: 32 (over x, y, core), replica: 16 (over z).
Axes of the slice: x: 4, y: 4, z: 16, core: 2. Of those that a mesh axis runs over, the one named last changes fastest.
Arguments:
- tokens: bfloat16 [65536, 2560], P(('expert', 'replica')), may hold values from -6 to 6
- cotangent: bfloat16 [65536, 2560], P(('expert', 'replica')), may hold values from -4 to 4
- partner: int32 [65536, 1], P(('expert', 'replica')), may hold values from 0 to 31; in each aligned block of 128 rows (0 to 127, 128 to 255, ...) at most 5 rows name the same one
- combine: int32 [65536, 2], P(('expert', 'replica')), may hold values from 1 to 8
- counts: int32 [512], P(('expert', 'replica')), may hold values from 32 to 128, as said below
- w_gate: bfloat16 [32, 2560, 768], P('expert', 'replica'), may hold values from -0.125 to 0.125
- w_up: bfloat16 [32, 2560, 768], P('expert', 'replica'), may hold values from -0.125 to 0.125
- w_down: bfloat16 [32, 768, 2560], P('expert', 'replica'), may hold values from -0.21875 to 0.21875
Outputs:
- token_grad: bfloat16 [65536, 2560], P(('expert', 'replica'))
- grad_down: bfloat16 [32, 768, 2560], P('expert', 'replica')
Inputs may be any that keep to these rules, and one draw needn't show every extreme that they name: `partner`: within the 128 rows of one device no expert index is named by more than 5 rows, and some device names one exactly 5 times. `counts`: some device has all 128 slots real.
All inputs are finite; a program needn't handle non-finite values.
Results may differ from a plain program's by a relative error of at most 0.017.
Values may be sent and summed in bfloat16 or wider, within the bound.
No kernel may reach another device: no remote copies, remote signals or barrier semaphores. Data moves between devices by JAX's collectives and lax.ppermute only.
A program may use at most 64 MiB of HBM per device.

v0:
```python
import jax
import jax.numpy as jnp
from jax import lax
from jax.sharding import PartitionSpec as P


def against_rows(left, matrix):
    return lax.dot_general(
        left, matrix, (((1,), (1,)), ((), ())), preferred_element_type=jnp.float32
    )


def expert_backward(inputs, upstream, gate_w, up_w, down_w):
    gate_act = jnp.dot(inputs, gate_w, preferred_element_type=jnp.float32)
    up_act = jnp.dot(inputs, up_w, preferred_element_type=jnp.float32)
    sigmoid_gate = jax.nn.sigmoid(gate_act)
    swish_gate = gate_act * sigmoid_gate
    hidden = (swish_gate * up_act).astype(jnp.bfloat16)
    hidden_grad = against_rows(upstream, down_w)
    gate_grad = (
        hidden_grad * up_act * sigmoid_gate * (1.0 + gate_act * (1.0 - sigmoid_gate))
    ).astype(jnp.bfloat16)
    up_grad = (hidden_grad * swish_gate).astype(jnp.bfloat16)
    input_grad = against_rows(gate_grad, gate_w) + against_rows(up_grad, up_w)
    return (hidden, input_grad)


def local(tokens, cotangent, partner, combine, counts, w_gate, w_up, w_down):
    tok_rows = tokens.shape[0]
    width = tokens.shape[1]
    expert_count = lax.axis_size("expert")
    capacity = max(2, (5 * tok_rows // 4 + expert_count - 1) // expert_count)
    positions = jnp.arange(tok_rows, dtype=jnp.int32)
    valid_rows = positions < counts[0]
    weights = combine.astype(jnp.float32)
    weight_sum = weights[:, 0] + weights[:, 1]
    share_home = jnp.where(valid_rows, weights[:, 0] / weight_sum, 0.0)
    share_away = jnp.where(valid_rows, weights[:, 1] / weight_sum, 0.0)
    upstream = cotangent.astype(jnp.float32)
    q_home = (upstream * share_home[:, None]).astype(jnp.bfloat16)
    q_away = (upstream * share_away[:, None]).astype(jnp.bfloat16)
    gate_full, up_full, down_full = (
        lax.all_gather(w_gate, "replica", axis=1, tiled=True),
        lax.all_gather(w_up, "replica", axis=1, tiled=True),
        lax.all_gather(w_down, "replica", axis=1, tiled=True),
    )
    gate_w = gate_full.reshape(gate_full.shape[1], gate_full.shape[2])
    up_w = up_full.reshape(up_full.shape[1], up_full.shape[2])
    down_w = down_full.reshape(down_full.shape[1], down_full.shape[2])
    target = partner[:, 0]
    onehot_rows = (target[:, None] == jnp.arange(expert_count, dtype=jnp.int32)[None, :]).astype(
        jnp.int32
    )
    rank_within = jnp.sum((jnp.cumsum(onehot_rows, axis=0) - onehot_rows) * onehot_rows, axis=1)
    destination = target * capacity + rank_within
    placing = (
        jnp.arange(expert_count * capacity, dtype=jnp.int32)[:, None] == destination[None, :]
    ).astype(jnp.bfloat16)
    send_x = (
        jnp.dot(placing, tokens, preferred_element_type=jnp.float32)
        .astype(jnp.bfloat16)
        .reshape(expert_count, capacity, width)
    )
    send_q = (
        jnp.dot(placing, q_away, preferred_element_type=jnp.float32)
        .astype(jnp.bfloat16)
        .reshape(expert_count, capacity, width)
    )
    hidden_home, grad_home = expert_backward(tokens, q_home, gate_w, up_w, down_w)
    x_there = lax.all_to_all(send_x, "expert", split_axis=0, concat_axis=0, tiled=True)
    q_there = lax.all_to_all(send_q, "expert", split_axis=0, concat_axis=0, tiled=True)
    item_count = x_there.shape[1]
    hidden_there, grad_there = expert_backward(
        x_there.reshape(-1, width), q_there.reshape(-1, width), gate_w, up_w, down_w
    )
    returned = lax.all_to_all(
        grad_there.astype(jnp.bfloat16).reshape(expert_count, item_count, width),
        "expert",
        split_axis=0,
        concat_axis=0,
        tiled=True,
    )
    returned, hidden_away, q_there = (
        returned,
        hidden_there.reshape(expert_count, item_count, -1),
        q_there,
    )
    contract = (((0,), (0,)), ((), ()))
    flat_returned = returned.reshape(expert_count * capacity, width)
    grad_away = lax.dot_general(
        placing, flat_returned, contract, preferred_element_type=jnp.float32
    )
    token_grad = (grad_home + grad_away).astype(jnp.bfloat16)
    flat_hidden = hidden_away.reshape(expert_count * capacity, -1)
    flat_q = q_there.reshape(expert_count * capacity, width)
    grad_down = lax.psum_scatter(
        (
            lax.dot_general(hidden_home, q_home, contract, preferred_element_type=jnp.float32)
            + lax.dot_general(flat_hidden, flat_q, contract, preferred_element_type=jnp.float32)
        ).astype(jnp.bfloat16),
        "replica",
        scatter_dimension=0,
        tiled=True,
    )
    return (token_grad, grad_down[None])


def solution(mesh):
    placed = (
        P(("expert", "replica"), None),
        P(("expert", "replica"), None),
        P(("expert", "replica"), None),
        P(("expert", "replica"), None),
        P(("expert", "replica")),
        P("expert", "replica", None),
        P("expert", "replica", None),
        P("expert", "replica", None),
    )
    return jax.shard_map(
        local,
        mesh=mesh,
        in_specs=placed,
        out_specs=(P(("expert", "replica"), None), P("expert", "replica", None)),
        check_vma=False,
    )
```

profile of v0, /device:TPU:10, one launch (start us, length us, event | category | flops | bytes accessed | tf_op | source)
XLA Modules:
  0.0 331.8 jit_solution(12413700207397267182)
XLA Ops:
  13.1 1.5 convolution_convert_fusion.1
  15.9 9.4 %all-to-all-start = ((bf16[32,5,2560]{2,1,0:T(8,128)(2,1)}), bf16[32,5,2560]{2,1,0:T(8,128)(2,1)S(1)}, u32[]{:S(2)}, u32[]{:S(2)}) async-start(bf16[32,5,2560]{2,1,0:T(8,128)(2,1)} %reshape.51), calls=%async_computation | async-start | bytes 2621440 | tf_op jit(solution)/shard_map/all_to_all | solution.py:71
  25.7 1.3 reshape.53
  27.1 15.6 %all-to-all-done = bf16[32,5,2560]{2,1,0:T(8,128)(2,1)S(1)} async-done(((bf16[32,5,2560]{2,1,0:T(8,128)(2,1)}), bf16[32,5,2560]{2,1,0:T(8,128)(2,1)S(1)}, u32[]{:S(2)}, u32[]{:S(2)}) %all-to-all-start) | async-done | bytes 819232 | tf_op jit(solution)/shard_map/all_to_all | solution.py:71
  42.7 7.1 %all-to-all-start.1 = ((bf16[32,5,2560]{2,1,0:T(8,128)(2,1)}), bf16[32,5,2560]{2,1,0:T(8,128)(2,1)}, u32[]{:S(2)}, u32[]{:S(2)}) async-start(bf16[32,5,2560]{2,1,0:T(8,128)(2,1)} %reshape.53), calls=%async_computation.1 | async-start | bytes 2621440 | tf_op jit(solution)/shard_map/all_to_all | solution.py:70
  50.2 16.9 %all-to-all-done.1 = bf16[32,5,2560]{2,1,0:T(8,128)(2,1)} async-done(((bf16[32,5,2560]{2,1,0:T(8,128)(2,1)}), bf16[32,5,2560]{2,1,0:T(8,128)(2,1)}, u32[]{:S(2)}, u32[]{:S(2)}) %all-to-all-start.1) | async-done | bytes 819232 | tf_op jit(solution)/shard_map/all_to_all | solution.py:70
  67.1 1.5 reshape.54
  68.6 23.4 %all-gather.8.cloned.1.call-done = bf16[1,2560,768]{2,1,0:T(8,128)(2,1)} async-done(((bf16[1,160,768]{2,1,0:T(8,128)(2,1)}), bf16[1,2560,768]{2,1,0:T(8,128)(2,1)}) %all-gather.8.cloned.1.call-update) | async-done | bytes 3932176 | tf_op jit(solution)/shard_map/all_gather | solution.py:43
  92.0 2.8 fusion.6
  94.8 73.8 %all-gather.6.cloned.1.call-done = bf16[1,2560,768]{2,1,0:T(8,128)(2,1)} async-done(((bf16[1,160,768]{2,1,0:T(8,128)(2,1)}), bf16[1,2560,768]{2,1,0:T(8,128)(2,1)}) %all-gather.6.cloned.1.call-update) | async-done | bytes 3932176 | tf_op jit(solution)/shard_map/all_gather | solution.py:44
  168.6 2.9 fusion.14
  171.6 3.1 fusion.2
  177.0 3.2 add_convert_fusion
  180.2 64.9 %all-gather.4.cloned.1.call-done = bf16[1,768,2560]{2,1,0:T(8,128)(2,1)} async-done(((bf16[1,48,2560]{2,1,0:T(8,128)(2,1)}), bf16[1,768,2560]{2,1,0:T(8,128)(2,1)}) %all-gather.4.cloned.1.call-update) | async-done | bytes 3932176 | tf_op jit(solution)/shard_map/all_gather | solution.py:45
  245.1 3.7 %fusion.16 = f32[160,768]{1,0:T(8,128)S(1)} fusion(bf16[160,2560]{1,0:T(8,128)(2,1)S(1)} %reshape.52, bf16[1,768,2560]{2,1,0:T(8,128)(2,1)} %all-gather.4.cloned.1.call-done), kind=kOutput, calls=%fused_computation.17 | convolution fusion | flops 629145600 | bytes 5242880 | tf_op jit(solution)/shard_map/dot_general | solution.py:8
  248.9 1.4 fusion
  251.0 1.4 fusion.26
  253.7 7.6 %all-to-all-start.2 = ((bf16[32,5,2560]{2,1,0:T(8,128)(2,1)}), bf16[32,5,2560]{2,1,0:T(8,128)(2,1)}, u32[]{:S(2)}, u32[]{:S(2)}) async-start(bf16[32,5,2560]{2,1,0:T(8,128)(2,1)} %reshape.55), calls=%async_computation.2 | async-start | bytes 2621440 | tf_op jit(solution)/shard_map/all_to_all | solution.py:76
  261.3 3.7 %fusion.18 = f32[128,768]{1,0:T(8,128)S(1)} fusion(bf16[1,768,2560]{2,1,0:T(8,128)(2,1)} %all-gather.4.cloned.1.call-done, bf16[128,2560]{1,0:T(8,128)(2,1)S(1)} %copy-done.7, f32[128]{0:T(128)S(1)} %get-tuple-element.3), kind=kOutput, calls=%fused_computation.19 | convolution fusion | flops 504299520 | bytes 4981248 | tf_op jit(solution)/shard_map/dot_general | solution.py:8
  265.0 1.4 fusion.4
  267.1 1.4 fusion.23
  268.5 10.0 %all-to-all-done.2 = bf16[32,5,2560]{2,1,0:T(8,128)(2,1)} async-done(((bf16[32,5,2560]{2,1,0:T(8,128)(2,1)}), bf16[32,5,2560]{2,1,0:T(8,128)(2,1)}, u32[]{:S(2)}, u32[]{:S(2)}) %all-to-all-start.2) | async-done | bytes 819232 | tf_op jit(solution)/shard_map/all_to_all | solution.py:76
  278.5 1.5 reshape.56
  281.2 44.0 %reduce-scatter.2.cloned.1.call-done = bf16[48,2560]{1,0:T(8,128)(2,1)} async-done(((bf16[768,2560]{1,0:T(8,128)(2,1)}), bf16[48,2560]{1,0:T(8,128)(2,1)}) %reduce-scatter.2.cloned.1.call-update) | async-done | bytes 245776 | tf_op jit(solution)/shard_map/reduce_scatter | solution.py:96
  (45 shorter events, 13.5 us)
Async XLA Ops:
  7.2 18.2 %copy-start = (bf16[128,2560]{1,0:T(8,128)(2,1)S(1)}, bf16[128,2560]{1,0:T(8,128)(2,1)}, u32[]{:S(2)}) copy-start(bf16[128,2560]{1,0:T(8,128)(2,1)} %param.8) | copy-start | bytes 1966084
  7.2 84.8 %all-gather.8.cloned.1.call-start = ((), (), s32[]{:S(2)}) async-start(), calls=%async_computation.6 | async-start | bytes 4177920 | tf_op jit(solution)/shard_map/all_gather | solution.py:43
  7.9 160.7 %all-gather.6.cloned.1.call-start = ((), (), s32[]{:S(2)}) async-start(), calls=%async_computation.5 | async-start | bytes 4177920 | tf_op jit(solution)/shard_map/all_gather | solution.py:44
  8.7 236.5 %all-gather.4.cloned.1.call-start = ((), (), s32[]{:S(2)}) async-start(), calls=%async_computation.4 | async-start | bytes 4177920 | tf_op jit(solution)/shard_map/all_gather | solution.py:45
  15.9 26.7 %all-to-all-start = ((bf16[32,5,2560]{2,1,0:T(8,128)(2,1)}), bf16[32,5,2560]{2,1,0:T(8,128)(2,1)S(1)}, u32[]{:S(2)}, u32[]{:S(2)}) async-start(bf16[32,5,2560]{2,1,0:T(8,128)(2,1)} %reshape.51), calls=%async_computation | async-start | bytes 2621440 | tf_op jit(solution)/shard_map/all_to_all | solution.py:71
  42.7 24.4 %all-to-all-start.1 = ((bf16[32,5,2560]{2,1,0:T(8,128)(2,1)}), bf16[32,5,2560]{2,1,0:T(8,128)(2,1)}, u32[]{:S(2)}, u32[]{:S(2)}) async-start(bf16[32,5,2560]{2,1,0:T(8,128)(2,1)} %reshape.53), calls=%async_computation.1 | async-start | bytes 2621440 | tf_op jit(solution)/shard_map/all_to_all | solution.py:70
  49.8 275.5 %reduce-scatter.2.cloned.1.call-start = ((), (), s32[]{:S(2)}) async-start(), calls=%async_computation.7 | async-start | bytes 4177920 | tf_op jit(solution)/shard_map/reduce_scatter | solution.py:96
  168.6 6.0 %copy-start.1 = (bf16[1,2560,768]{2,1,0:T(8,128)(2,1)S(1)}, bf16[1,2560,768]{2,1,0:T(8,128)(2,1)}, u32[]{:S(2)}) copy-start(bf16[1,2560,768]{2,1,0:T(8,128)(2,1)} %all-gather.6.cloned.1.call-done) | copy-start | bytes 11796484
  171.5 3.9 %copy-start.10 = (f32[128,768]{1,0:T(8,128)}, f32[128,768]{1,0:T(8,128)S(1)}, u32[]{:S(2)}) copy-start(f32[128,768]{1,0:T(8,128)S(1)} %fusion.14) | copy-start | bytes 1179652
  174.6 1.1 copy-start.6
  175.4 1.6 copy-start.8
  180.2 68.6 %copy-start.9 = (f32[160,768]{1,0:T(8,128)S(1)}, f32[160,768]{1,0:T(8,128)}, u32[]{:S(2)}) copy-start(f32[160,768]{1,0:T(8,128)} %copy-done.8) | copy-start | bytes 1474564
  245.1 3.7 %copy-start.4 = (bf16[1,2560,768]{2,1,0:T(8,128)(2,1)S(1)}, bf16[1,2560,768]{2,1,0:T(8,128)(2,1)}, u32[]{:S(2)}) copy-start(bf16[1,2560,768]{2,1,0:T(8,128)(2,1)} %all-gather.8.cloned.1.call-done) | copy-start | bytes 11796484
  248.9 2.1 copy-start.2
  252.4 8.9 %copy-start.7 = (bf16[128,2560]{1,0:T(8,128)(2,1)S(1)}, bf16[128,2560]{1,0:T(8,128)(2,1)}, u32[]{:S(2)}) copy-start(bf16[128,2560]{1,0:T(8,128)(2,1)} %param.9) | copy-start | bytes 1966084
  253.7 11.3 %copy-start.11 = (f32[128,768]{1,0:T(8,128)S(1)}, f32[128,768]{1,0:T(8,128)}, u32[]{:S(2)}) copy-start(f32[128,768]{1,0:T(8,128)} %copy-done.10) | copy-start | bytes 1179652
  253.7 24.9 %all-to-all-start.2 = ((bf16[32,5,2560]{2,1,0:T(8,128)(2,1)}), bf16[32,5,2560]{2,1,0:T(8,128)(2,1)}, u32[]{:S(2)}, u32[]{:S(2)}) async-start(bf16[32,5,2560]{2,1,0:T(8,128)(2,1)} %reshape.55), calls=%async_computation.2 | async-start | bytes 2621440 | tf_op jit(solution)/shard_map/all_to_all | solution.py:76
  261.3 3.7 %copy-start.5 = (bf16[1,2560,768]{2,1,0:T(8,128)(2,1)S(1)}, bf16[1,2560,768]{2,1,0:T(8,128)(2,1)}, u32[]{:S(2)}) copy-start(bf16[1,2560,768]{2,1,0:T(8,128)(2,1)} %all-gather.8.cloned.1.call-done) | copy-start | bytes 11796484
  265.0 2.1 copy-start.3
Sparse Core Ops, SparseCore 0:
  10.1 81.8 all-gather.7
  94.1 74.4 all-gather.5
  170.7 74.4 all-gather.3
  248.4 76.7 reduce-scatter.1
where the time goes:
time: 333 us; the launch traced here: 332 us
  waiting for transfers between devices  251 us (75%)
  matrix products  30.2 us (9%)
  starting transfers between devices  24.2 us (7%)
  between operations  14.7 us (4%)
  local copies, waits for them, and re-layouts  8.84 us (3%)
    all_gather x1, waiting for transfers between devices, local(): lax.all_gather(w_up, 'replica', axis=1, tiled=True)  73.8 us
    all_gather x1, waiting for transfers between devices, local(): lax.all_gather(w_down, 'replica', axis=1, tiled=True)  64.9 us
    reduce_scatter x1, waiting for transfers between devices, local(): lax.psum_scatter((lax.dot_general(hidden_home, q_home, contract, preferre...  44 us
    all_gather x1, waiting for transfers between devices, local(): lax.all_gather(w_gate, 'replica', axis=1, tiled=True)  23.4 us
    all_to_all x1, waiting for transfers between devices, local(): lax.all_to_all(send_x, 'expert', split_axis=0, concat_axis=0, tiled=True)  16.9 us
    all_to_all x1, waiting for transfers between devices, local(): lax.all_to_all(send_q, 'expert', split_axis=0, concat_axis=0, tiled=True)  15.6 us
    dot_general x6, matrix products, against_rows(): lax.dot_general(left, matrix, (((1,), (1,)), ((), ())), preferred_element...  13 us
    all_to_all x1, waiting for transfers between devices, local(): lax.all_to_all(grad_there.astype(jnp.bfloat16).reshape(expert_count, item...  9.99 us
  transfers between devices with their start and end apart: 7, of which 7 were waited for; matrix products, arithmetic and copies ran while one was open for 12% of the time, Pallas kernels for 0%

commit v1 on v0

--- a/solution.py
+++ b/solution.py
@@ -39,8 +39,32 @@
     upstream = cotangent.astype(jnp.float32)
     q_home = (upstream * share_home[:, None]).astype(jnp.bfloat16)
     q_away = (upstream * share_away[:, None]).astype(jnp.bfloat16)
+
+    def treat_group_up(vals, dim_at=1):
+        axis_name = "replica"
+        z_new = lax.axis_size(axis_name)
+        after = lax.axis_index(axis_name)
+        y1, tile_out, part_next = (z_new, after, vals.shape[dim_at])
+        leaves = tuple((i0 * y1 if w == dim_at else i0 for w, i0 in enumerate(vals.shape)))
+        f_now = jnp.zeros(leaves, vals.dtype)
+        right_arr = inter = vals
+        o_now = lax.dynamic_update_slice_in_dim(f_now, vals, tile_out * part_next, axis=dim_at)
+        for b in range(1, y1 // 2 + 1):
+            even = tuple(((w, (w + 1) % y1) for w in range(y1)))
+            right_arr = lax.ppermute(right_arr, axis_name, even)
+            o_now = lax.dynamic_update_slice_in_dim(
+                o_now, right_arr, (tile_out - b) % y1 * part_next, axis=dim_at
+            )
+            if 2 * b < y1:
+                block_last = tuple(((w, (w - 1) % y1) for w in range(y1)))
+                inter = lax.ppermute(inter, axis_name, block_last)
+                o_now = lax.dynamic_update_slice_in_dim(
+                    o_now, inter, (tile_out + b) % y1 * part_next, axis=dim_at
+                )
+        return o_now
+
     gate_full, up_full, down_full = (
-        lax.all_gather(w_gate, "replica", axis=1, tiled=True),
+        treat_group_up(w_gate),
         lax.all_gather(w_up, "replica", axis=1, tiled=True),
         lax.all_gather(w_down, "replica", axis=1, tiled=True),
     )

time: 333 us -> 268 us (0.80)
  the two profiles are of different devices: /device:TPU:10 before, /device:TPU:6 now
where the time goes in v1:
time: 268 us; the launch traced here: 267 us
  waiting for transfers between devices  109 us (41%)
  starting transfers between devices  80 us (30%)
  matrix products  37 us (14%)
  local copies, waits for them, and re-layouts  22.5 us (8%)
  between operations  15.1 us (6%)
  other arithmetic  3.09 us (1%)
    ppermute x7, starting transfers between devices, treat_group_up(): inter = lax.ppermute(inter, axis_name, block_last)  40.3 us
    reduce_scatter x1, waiting for transfers between devices, local(): lax.psum_scatter((lax.dot_general(hidden_home, q_home, contract, preferre...  36.4 us
    ppermute x8, waiting for transfers between devices, treat_group_up(): right_arr = lax.ppermute(right_arr, axis_name, even)  26.9 us
    all_gather x1, waiting for transfers between devices, local(): lax.all_gather(w_down, 'replica', axis=1, tiled=True)  24.9 us
    dot_general x6, matrix products, against_rows(): lax.dot_general(left, matrix, (((1,), (1,)), ((), ())), preferred_element...  19.6 us
    ppermute x8, starting transfers between devices, treat_group_up(): right_arr = lax.ppermute(right_arr, axis_name, even)  17.4 us
    all_to_all x1, waiting for transfers between devices, local(): lax.all_to_all(grad_there.astype(jnp.bfloat16).reshape(expert_count, item...  11.2 us
    all_to_all x1, waiting for transfers between devices, local(): lax.all_to_all(send_x, 'expert', split_axis=0, concat_axis=0, tiled=True)  7.77 us
  transfers between devices with their start and end apart: 21, of which 10 were waited for; matrix products, arithmetic and copies ran while one was open for 23% of the time, Pallas kernels for 0%

profile of v1, /device:TPU:6, one launch (start us, length us, event | category | flops | bytes accessed | tf_op | source)
XLA Modules:
  0.0 266.6 jit_solution(12055366261940696526)
XLA Ops:
  8.0 3.8 %collective-permute-start = (bf16[1,160,768]{2,1,0:T(8,128)(2,1)}, bf16[1,160,768]{2,1,0:T(8,128)(2,1)S(1)}, u32[]{:S(2)}, u32[]{:S(2)}) collective-permute-start(bf16[1,160,768]{2,1,0:T(8,128)(2,1)} %param.13), channel_id=1, source_target_pairs={{0,1},{1,2},{2,3},{3,4},{4,5},{5,6},{6,7},{7,8},{8,9},{9,10},{10,1... | collective-permute-start | bytes 737288 | tf_op jit(solution)/shard_map/ppermute | solution.py:54
  11.8 9.5 %collective-permute-start.1 = (bf16[1,160,768]{2,1,0:T(8,128)(2,1)}, bf16[1,160,768]{2,1,0:T(8,128)(2,1)S(1)}, u32[]{:S(2)}, u32[]{:S(2)}) collective-permute-start(bf16[1,160,768]{2,1,0:T(8,128)(2,1)} %param.13), channel_id=1, source_target_pairs={{0,15},{1,0},{2,1},{3,2},{4,3},{5,4},{6,5},{7,6},{8,7},{9,8},{10,9... | collective-permute-start | bytes 737288 | tf_op jit(solution)/shard_map/ppermute | solution.py:60
  27.9 7.6 %all-to-all-start = ((bf16[32,5,2560]{2,1,0:T(8,128)(2,1)}), bf16[32,5,2560]{2,1,0:T(8,128)(2,1)S(1)}, u32[]{:S(2)}, u32[]{:S(2)}) async-start(bf16[32,5,2560]{2,1,0:T(8,128)(2,1)} %reshape.131), calls=%async_computation | async-start | bytes 2621440 | tf_op jit(solution)/shard_map/all_to_all | solution.py:95
  42.3 5.1 %collective-permute-start.3 = (bf16[1,160,768]{2,1,0:T(8,128)(2,1)S(1)}, bf16[1,160,768]{2,1,0:T(8,128)(2,1)S(1)}, u32[]{:S(2)}, u32[]{:S(2)}) collective-permute-start(bf16[1,160,768]{2,1,0:T(8,128)(2,1)S(1)} %collective-permute-done.1), channel_id=1, source_target_pairs={{0,15},{1,0},{2,1},{3,2},{4,3},{5,4},{6,5},{7,6},{8,7},{9,8},{10,9... | collective-permute-start | bytes 737288 | tf_op jit(solution)/shard_map/ppermute | solution.py:60
  48.8 7.4 %collective-permute-done.2 = bf16[1,160,768]{2,1,0:T(8,128)(2,1)S(1)} collective-permute-done((bf16[1,160,768]{2,1,0:T(8,128)(2,1)S(1)}, bf16[1,160,768]{2,1,0:T(8,128)(2,1)S(1)}, u32[]{:S(2)}, u32[]{:S(2)}) %collective-permute-start.2) | collective-permute-done | bytes 245792 | tf_op jit(solution)/shard_map/ppermute | solution.py:54
  58.1 5.1 %collective-permute-start.5 = (bf16[1,160,768]{2,1,0:T(8,128)(2,1)S(1)}, bf16[1,160,768]{2,1,0:T(8,128)(2,1)S(1)}, u32[]{:S(2)}, u32[]{:S(2)}) collective-permute-start(bf16[1,160,768]{2,1,0:T(8,128)(2,1)S(1)} %collective-permute-done.3), channel_id=1, source_target_pairs={{0,15},{1,0},{2,1},{3,2},{4,3},{5,4},{6,5},{7,6},{8,7},{9,8},{10,9... | collective-permute-start | bytes 737288 | tf_op jit(solution)/shard_map/ppermute | solution.py:60
  63.2 7.3 %all-to-all-start.1 = ((bf16[32,5,2560]{2,1,0:T(8,128)(2,1)}), bf16[32,5,2560]{2,1,0:T(8,128)(2,1)}, u32[]{:S(2)}, u32[]{:S(2)}) async-start(bf16[32,5,2560]{2,1,0:T(8,128)(2,1)} %reshape.133), calls=%async_computation.1 | async-start | bytes 2621440 | tf_op jit(solution)/shard_map/all_to_all | solution.py:94
  73.9 5.1 %collective-permute-start.7 = (bf16[1,160,768]{2,1,0:T(8,128)(2,1)S(1)}, bf16[1,160,768]{2,1,0:T(8,128)(2,1)}, u32[]{:S(2)}, u32[]{:S(2)}) collective-permute-start(bf16[1,160,768]{2,1,0:T(8,128)(2,1)S(1)} %collective-permute-done.5), channel_id=1, source_target_pairs={{0,15},{1,0},{2,1},{3,2},{4,3},{5,4},{6,5},{7,6},{8,7},{9,8},{10,9... | collective-permute-start | bytes 737288 | tf_op jit(solution)/shard_map/ppermute | solution.py:60
  80.9 7.8 %all-to-all-done.1 = bf16[32,5,2560]{2,1,0:T(8,128)(2,1)} async-done(((bf16[32,5,2560]{2,1,0:T(8,128)(2,1)}), bf16[32,5,2560]{2,1,0:T(8,128)(2,1)}, u32[]{:S(2)}, u32[]{:S(2)}) %all-to-all-start.1) | async-done | bytes 819232 | tf_op jit(solution)/shard_map/all_to_all | solution.py:94
  92.1 5.1 %collective-permute-start.9 = (bf16[1,160,768]{2,1,0:T(8,128)(2,1)}, bf16[1,160,768]{2,1,0:T(8,128)(2,1)S(1)}, u32[]{:S(2)}, u32[]{:S(2)}) collective-permute-start(bf16[1,160,768]{2,1,0:T(8,128)(2,1)} %collective-permute-done.7), channel_id=1, source_target_pairs={{0,15},{1,0},{2,1},{3,2},{4,3},{5,4},{6,5},{7,6},{8,7},{9,8},{10,9... | collective-permute-start | bytes 737288 | tf_op jit(solution)/shard_map/ppermute | solution.py:60
  99.7 3.3 %collective-permute-done.8 = bf16[1,160,768]{2,1,0:T(8,128)(2,1)S(1)} collective-permute-done((bf16[1,160,768]{2,1,0:T(8,128)(2,1)S(1)}, bf16[1,160,768]{2,1,0:T(8,128)(2,1)S(1)}, u32[]{:S(2)}, u32[]{:S(2)}) %collective-permute-start.8) | collective-permute-done | bytes 245792 | tf_op jit(solution)/shard_map/ppermute | solution.py:54
  104.8 5.1 %collective-permute-start.11 = (bf16[1,160,768]{2,1,0:T(8,128)(2,1)S(1)}, bf16[1,160,768]{2,1,0:T(8,128)(2,1)S(1)}, u32[]{:S(2)}, u32[]{:S(2)}) collective-permute-start(bf16[1,160,768]{2,1,0:T(8,128)(2,1)S(1)} %collective-permute-done.9), channel_id=1, source_target_pairs={{0,15},{1,0},{2,1},{3,2},{4,3},{5,4},{6,5},{7,6},{8,7},{9,8},{10,9... | collective-permute-start | bytes 737288 | tf_op jit(solution)/shard_map/ppermute | solution.py:60
  115.3 5.1 %collective-permute-start.13 = (bf16[1,160,768]{2,1,0:T(8,128)(2,1)S(1)}, bf16[1,160,768]{2,1,0:T(8,128)(2,1)S(1)}, u32[]{:S(2)}, u32[]{:S(2)}) collective-permute-start(bf16[1,160,768]{2,1,0:T(8,128)(2,1)S(1)} %collective-permute-done.11), channel_id=1, source_target_pairs={{0,15},{1,0},{2,1},{3,2},{4,3},{5,4},{6,5},{7,6},{8,7},{9,8},{10,9... | collective-permute-start | bytes 737288 | tf_op jit(solution)/shard_map/ppermute | solution.py:60
  121.9 4.2 %collective-permute-done.12 = bf16[1,160,768]{2,1,0:T(8,128)(2,1)S(1)} collective-permute-done((bf16[1,160,768]{2,1,0:T(8,128)(2,1)S(1)}, bf16[1,160,768]{2,1,0:T(8,128)(2,1)S(1)}, u32[]{:S(2)}, u32[]{:S(2)}) %collective-permute-start.12) | collective-permute-done | bytes 245792 | tf_op jit(solution)/shard_map/ppermute | solution.py:54
  130.5 10.1 %collective-permute-done.14 = bf16[1,160,768]{2,1,0:T(8,128)(2,1)S(1)} collective-permute-done((bf16[1,160,768]{2,1,0:T(8,128)(2,1)S(1)}, bf16[1,160,768]{2,1,0:T(8,128)(2,1)S(1)}, u32[]{:S(2)}, u32[]{:S(2)}) %collective-permute-start.14) | collective-permute-done | bytes 245792 | tf_op jit(solution)/shard_map/ppermute | solution.py:54
  152.7 3.2 %add_convert_fusion = bf16[768,2560]{1,0:T(8,128)(2,1)} fusion(f32[768,2560]{1,0:T(8,128)S(1)} %fusion.21, bf16[160,2560]{1,0:T(8,128)(2,1)S(1)} %reshape.132, f32[160,768]{1,0:T(8,128)S(1)} %fusion.2, f32[160,768]{1,0:T(8,128)S(1)} %fusion.43), kind=kOutput, calls=%fused_computation | convolution fusion | flops 633815040 | bytes 13598720 | tf_op jit(solution)/shard_map/dot_general | solution.py:123
  155.8 24.9 %all-gather.3.cloned.1.call-done = bf16[1,768,2560]{2,1,0:T(8,128)(2,1)} async-done(((bf16[1,48,2560]{2,1,0:T(8,128)(2,1)}), bf16[1,768,2560]{2,1,0:T(8,128)(2,1)}) %all-gather.3.cloned.1.call-update) | async-done | bytes 3932176 | tf_op jit(solution)/shard_map/all_gather | solution.py:69
  180.7 3.7 %fusion.8 = f32[160,768]{1,0:T(8,128)S(1)} fusion(bf16[160,2560]{1,0:T(8,128)(2,1)S(1)} %reshape.132, bf16[1,768,2560]{2,1,0:T(8,128)(2,1)} %all-gather.3.cloned.1.call-done), kind=kOutput, calls=%fused_computation.9 | convolution fusion | flops 629145600 | bytes 5242880 | tf_op jit(solution)/shard_map/dot_general | solution.py:8
  185.8 3.6 %fusion.13 = bf16[160,2560]{1,0:T(8,128)(2,1)S(1)} fusion(f32[160,2560]{1,0:T(8,128)S(1)} %fusion, bf16[2560,768]{1,0:T(8,128)(2,1)} %bitcast_dynamic-update-slice_fusion, f32[160,768]{1,0:T(8,128)S(1)} %fusion.43, f32[160,768]{1,0:T(8,128)S(1)} %fusion.8, f32[160,768]{1,0:T(8,128)S(1)} %copy-done.7), kind=kOutput, calls=%fused_computation.16 | convolution fusion | flops 631193600 | bytes 7864320 | tf_op jit(solution)/shard_map/dot_general | solution.py:8
  190.7 7.4 %all-to-all-start.2 = ((bf16[32,5,2560]{2,1,0:T(8,128)(2,1)}), bf16[32,5,2560]{2,1,0:T(8,128)(2,1)S(1)}, u32[]{:S(2)}, u32[]{:S(2)}) async-start(bf16[32,5,2560]{2,1,0:T(8,128)(2,1)} %reshape.135), calls=%async_computation.2 | async-start | bytes 2621440 | tf_op jit(solution)/shard_map/all_to_all | solution.py:100
  198.1 3.7 %fusion.10 = f32[128,768]{1,0:T(8,128)S(1)} fusion(bf16[1,768,2560]{2,1,0:T(8,128)(2,1)} %all-gather.3.cloned.1.call-done, bf16[128,2560]{1,0:T(8,128)(2,1)S(1)} %copy-done.5, f32[128]{0:T(128)S(1)} %get-tuple-element.2), kind=kOutput, calls=%fused_computation.11 | convolution fusion | flops 504299520 | bytes 4981248 | tf_op jit(solution)/shard_map/dot_general | solution.py:8
  205.0 11.2 %all-to-all-done.2 = bf16[32,5,2560]{2,1,0:T(8,128)(2,1)S(1)} async-done(((bf16[32,5,2560]{2,1,0:T(8,128)(2,1)}), bf16[32,5,2560]{2,1,0:T(8,128)(2,1)S(1)}, u32[]{:S(2)}, u32[]{:S(2)}) %all-to-all-start.2) | async-done | bytes 819232 | tf_op jit(solution)/shard_map/all_to_all | solution.py:100
  218.8 4.8 %fusion.14 = bf16[128,2560]{1,0:T(8,128)(2,1)} fusion(f32[128,2560]{1,0:T(8,128)S(1)} %fusion.28, f32[128,2560]{1,0:T(8,128)} %fusion.4, bf16[2560,768]{1,0:T(8,128)(2,1)} %bitcast_dynamic-update-slice_fusion, f32[128,768]{1,0:T(8,128)S(1)} %convolution_bitcast_fusion, f32[128,768]{1,0:T(8,128)S(1)} %copy-done.11, f32[128,768]{1,0:T(8,128)S(1)} %copy-done.9), kind=kOutput, calls=%fused_computation.19 | convolution fusion | flops 505282560 | bytes 8388608 | tf_op jit(solution)/shard_map/dot_general | solution.py:8
  223.7 36.4 %reduce-scatter.2.cloned.1.call-done = bf16[48,2560]{1,0:T(8,128)(2,1)} async-done(((bf16[768,2560]{1,0:T(8,128)(2,1)}), bf16[48,2560]{1,0:T(8,128)(2,1)}) %reduce-scatter.2.cloned.1.call-update) | async-done | bytes 245776 | tf_op jit(solution)/shard_map/reduce_scatter | solution.py:120
  (91 shorter events, 61.1 us)
Async XLA Ops:
  7.2 28.4 %copy-start = (bf16[128,2560]{1,0:T(8,128)(2,1)S(1)}, bf16[128,2560]{1,0:T(8,128)(2,1)}, u32[]{:S(2)}) copy-start(bf16[128,2560]{1,0:T(8,128)(2,1)} %param.8) | copy-start | bytes 1966084
  7.2 140.0 %all-gather.5.cloned.1.call-start = ((), (), s32[]{:S(2)}) async-start(), calls=%async_computation.5 | async-start | bytes 4177920 | tf_op jit(solution)/shard_map/all_gather | solution.py:68
  7.9 172.8 %all-gather.3.cloned.1.call-start = ((), (), s32[]{:S(2)}) async-start(), calls=%async_computation.4 | async-start | bytes 4177920 | tf_op jit(solution)/shard_map/all_gather | solution.py:69
  8.0 32.4 %collective-permute-start = (bf16[1,160,768]{2,1,0:T(8,128)(2,1)}, bf16[1,160,768]{2,1,0:T(8,128)(2,1)S(1)}, u32[]{:S(2)}, u32[]{:S(2)}) collective-permute-start(bf16[1,160,768]{2,1,0:T(8,128)(2,1)} %param.13), channel_id=1, source_target_pairs={{0,1},{1,2},{2,3},{3,4},{4,5},{5,6},{6,7},{7,8},{8,9},{9,10},{10,1... | collective-permute-start | bytes 737288 | tf_op jit(solution)/shard_map/ppermute | solution.py:54
  11.8 30.5 %collective-permute-start.1 = (bf16[1,160,768]{2,1,0:T(8,128)(2,1)}, bf16[1,160,768]{2,1,0:T(8,128)(2,1)S(1)}, u32[]{:S(2)}, u32[]{:S(2)}) collective-permute-start(bf16[1,160,768]{2,1,0:T(8,128)(2,1)} %param.13), channel_id=1, source_target_pairs={{0,15},{1,0},{2,1},{3,2},{4,3},{5,4},{6,5},{7,6},{8,7},{9,8},{10,9... | collective-permute-start | bytes 737288 | tf_op jit(solution)/shard_map/ppermute | solution.py:60
  27.9 35.3 %all-to-all-start = ((bf16[32,5,2560]{2,1,0:T(8,128)(2,1)}), bf16[32,5,2560]{2,1,0:T(8,128)(2,1)S(1)}, u32[]{:S(2)}, u32[]{:S(2)}) async-start(bf16[32,5,2560]{2,1,0:T(8,128)(2,1)} %reshape.131), calls=%async_computation | async-start | bytes 2621440 | tf_op jit(solution)/shard_map/all_to_all | solution.py:95
  40.3 15.8 %collective-permute-start.2 = (bf16[1,160,768]{2,1,0:T(8,128)(2,1)S(1)}, bf16[1,160,768]{2,1,0:T(8,128)(2,1)S(1)}, u32[]{:S(2)}, u32[]{:S(2)}) collective-permute-start(bf16[1,160,768]{2,1,0:T(8,128)(2,1)S(1)} %collective-permute-done), channel_id=1, source_target_pairs={{0,1},{1,2},{2,3},{3,4},{4,5},{5,6},{6,7},{7,8},{8,9},{9,10},{10,1... | collective-permute-start | bytes 737288 | tf_op jit(solution)/shard_map/ppermute | solution.py:54
  42.3 15.8 %collective-permute-start.3 = (bf16[1,160,768]{2,1,0:T(8,128)(2,1)S(1)}, bf16[1,160,768]{2,1,0:T(8,128)(2,1)S(1)}, u32[]{:S(2)}, u32[]{:S(2)}) collective-permute-start(bf16[1,160,768]{2,1,0:T(8,128)(2,1)S(1)} %collective-permute-done.1), channel_id=1, source_target_pairs={{0,15},{1,0},{2,1},{3,2},{4,3},{5,4},{6,5},{7,6},{8,7},{9,8},{10,9... | collective-permute-start | bytes 737288 | tf_op jit(solution)/shard_map/ppermute | solution.py:60
  56.2 15.8 %collective-permute-start.4 = (bf16[1,160,768]{2,1,0:T(8,128)(2,1)S(1)}, bf16[1,160,768]{2,1,0:T(8,128)(2,1)S(1)}, u32[]{:S(2)}, u32[]{:S(2)}) collective-permute-start(bf16[1,160,768]{2,1,0:T(8,128)(2,1)S(1)} %collective-permute-done.2), channel_id=1, source_target_pairs={{0,1},{1,2},{2,3},{3,4},{4,5},{5,6},{6,7},{7,8},{8,9},{9,10},{10,1... | collective-permute-start | bytes 737288 | tf_op jit(solution)/shard_map/ppermute | solution.py:54
  58.1 15.8 %collective-permute-start.5 = (bf16[1,160,768]{2,1,0:T(8,128)(2,1)S(1)}, bf16[1,160,768]{2,1,0:T(8,128)(2,1)S(1)}, u32[]{:S(2)}, u32[]{:S(2)}) collective-permute-start(bf16[1,160,768]{2,1,0:T(8,128)(2,1)S(1)} %collective-permute-done.3), channel_id=1, source_target_pairs={{0,15},{1,0},{2,1},{3,2},{4,3},{5,4},{6,5},{7,6},{8,7},{9,8},{10,9... | collective-permute-start | bytes 737288 | tf_op jit(solution)/shard_map/ppermute | solution.py:60
  63.2 25.4 %all-to-all-start.1 = ((bf16[32,5,2560]{2,1,0:T(8,128)(2,1)}), bf16[32,5,2560]{2,1,0:T(8,128)(2,1)}, u32[]{:S(2)}, u32[]{:S(2)}) async-start(bf16[32,5,2560]{2,1,0:T(8,128)(2,1)} %reshape.133), calls=%async_computation.1 | async-start | bytes 2621440 | tf_op jit(solution)/shard_map/all_to_all | solution.py:94
  70.5 189.5 %reduce-scatter.2.cloned.1.call-start = ((), (), s32[]{:S(2)}) async-start(), calls=%async_computation.6 | async-start | bytes 4177920 | tf_op jit(solution)/shard_map/reduce_scatter | solution.py:120
  72.0 18.2 %collective-permute-start.6 = (bf16[1,160,768]{2,1,0:T(8,128)(2,1)S(1)}, bf16[1,160,768]{2,1,0:T(8,128)(2,1)S(1)}, u32[]{:S(2)}, u32[]{:S(2)}) collective-permute-start(bf16[1,160,768]{2,1,0:T(8,128)(2,1)S(1)} %collective-permute-done.4), channel_id=1, source_target_pairs={{0,1},{1,2},{2,3},{3,4},{4,5},{5,6},{6,7},{7,8},{8,9},{9,10},{10,1... | collective-permute-start | bytes 737288 | tf_op jit(solution)/shard_map/ppermute | solution.py:54
  73.9 18.2 %collective-permute-start.7 = (bf16[1,160,768]{2,1,0:T(8,128)(2,1)S(1)}, bf16[1,160,768]{2,1,0:T(8,128)(2,1)}, u32[]{:S(2)}, u32[]{:S(2)}) collective-permute-start(bf16[1,160,768]{2,1,0:T(8,128)(2,1)S(1)} %collective-permute-done.5), channel_id=1, source_target_pairs={{0,15},{1,0},{2,1},{3,2},{4,3},{5,4},{6,5},{7,6},{8,7},{9,8},{10,9... | collective-permute-start | bytes 737288 | tf_op jit(solution)/shard_map/ppermute | solution.py:60
  90.2 12.7 %collective-permute-start.8 = (bf16[1,160,768]{2,1,0:T(8,128)(2,1)S(1)}, bf16[1,160,768]{2,1,0:T(8,128)(2,1)S(1)}, u32[]{:S(2)}, u32[]{:S(2)}) collective-permute-start(bf16[1,160,768]{2,1,0:T(8,128)(2,1)S(1)} %collective-permute-done.6), channel_id=1, source_target_pairs={{0,1},{1,2},{2,3},{3,4},{4,5},{5,6},{6,7},{7,8},{8,9},{9,10},{10,1... | collective-permute-start | bytes 737288 | tf_op jit(solution)/shard_map/ppermute | solution.py:54
  92.1 12.7 %collective-permute-start.9 = (bf16[1,160,768]{2,1,0:T(8,128)(2,1)}, bf16[1,160,768]{2,1,0:T(8,128)(2,1)S(1)}, u32[]{:S(2)}, u32[]{:S(2)}) collective-permute-start(bf16[1,160,768]{2,1,0:T(8,128)(2,1)} %collective-permute-done.7), channel_id=1, source_target_pairs={{0,15},{1,0},{2,1},{3,2},{4,3},{5,4},{6,5},{7,6},{8,7},{9,8},{10,9... | collective-permute-start | bytes 737288 | tf_op jit(solution)/shard_map/ppermute | solution.py:60
  102.9 10.5 %collective-permute-start.10 = (bf16[1,160,768]{2,1,0:T(8,128)(2,1)S(1)}, bf16[1,160,768]{2,1,0:T(8,128)(2,1)S(1)}, u32[]{:S(2)}, u32[]{:S(2)}) collective-permute-start(bf16[1,160,768]{2,1,0:T(8,128)(2,1)S(1)} %collective-permute-done.8), channel_id=1, source_target_pairs={{0,1},{1,2},{2,3},{3,4},{4,5},{5,6},{6,7},{7,8},{8,9},{9,10},{10,1... | collective-permute-start | bytes 737288 | tf_op jit(solution)/shard_map/ppermute | solution.py:54
  104.8 10.5 %collective-permute-start.11 = (bf16[1,160,768]{2,1,0:T(8,128)(2,1)S(1)}, bf16[1,160,768]{2,1,0:T(8,128)(2,1)S(1)}, u32[]{:S(2)}, u32[]{:S(2)}) collective-permute-start(bf16[1,160,768]{2,1,0:T(8,128)(2,1)S(1)} %collective-permute-done.9), channel_id=1, source_target_pairs={{0,15},{1,0},{2,1},{3,2},{4,3},{5,4},{6,5},{7,6},{8,7},{9,8},{10,9... | collective-permute-start | bytes 737288 | tf_op jit(solution)/shard_map/ppermute | solution.py:60
  113.4 12.7 %collective-permute-start.12 = (bf16[1,160,768]{2,1,0:T(8,128)(2,1)S(1)}, bf16[1,160,768]{2,1,0:T(8,128)(2,1)S(1)}, u32[]{:S(2)}, u32[]{:S(2)}) collective-permute-start(bf16[1,160,768]{2,1,0:T(8,128)(2,1)S(1)} %collective-permute-done.10), channel_id=1, source_target_pairs={{0,1},{1,2},{2,3},{3,4},{4,5},{5,6},{6,7},{7,8},{8,9},{9,10},{10,1... | collective-permute-start | bytes 737288 | tf_op jit(solution)/shard_map/ppermute | solution.py:54
  115.3 14.5 %collective-permute-start.13 = (bf16[1,160,768]{2,1,0:T(8,128)(2,1)S(1)}, bf16[1,160,768]{2,1,0:T(8,128)(2,1)S(1)}, u32[]{:S(2)}, u32[]{:S(2)}) collective-permute-start(bf16[1,160,768]{2,1,0:T(8,128)(2,1)S(1)} %collective-permute-done.11), channel_id=1, source_target_pairs={{0,15},{1,0},{2,1},{3,2},{4,3},{5,4},{6,5},{7,6},{8,7},{9,8},{10,9... | collective-permute-start | bytes 737288 | tf_op jit(solution)/shard_map/ppermute | solution.py:60
  126.1 14.6 %collective-permute-start.14 = (bf16[1,160,768]{2,1,0:T(8,128)(2,1)S(1)}, bf16[1,160,768]{2,1,0:T(8,128)(2,1)S(1)}, u32[]{:S(2)}, u32[]{:S(2)}) collective-permute-start(bf16[1,160,768]{2,1,0:T(8,128)(2,1)S(1)} %collective-permute-done.12), channel_id=1, source_target_pairs={{0,1},{1,2},{2,3},{3,4},{4,5},{5,6},{6,7},{7,8},{8,9},{9,10},{10,1... | collective-permute-start | bytes 737288 | tf_op jit(solution)/shard_map/ppermute | solution.py:54
  190.7 25.5 %all-to-all-start.2 = ((bf16[32,5,2560]{2,1,0:T(8,128)(2,1)}), bf16[32,5,2560]{2,1,0:T(8,128)(2,1)S(1)}, u32[]{:S(2)}, u32[]{:S(2)}) async-start(bf16[32,5,2560]{2,1,0:T(8,128)(2,1)} %reshape.135), calls=%async_computation.2 | async-start | bytes 2621440 | tf_op jit(solution)/shard_map/all_to_all | solution.py:100
  202.5 16.3 %copy-start.9 = (f32[128,768]{1,0:T(8,128)S(1)}, f32[128,768]{1,0:T(8,128)}, u32[]{:S(2)}) copy-start(f32[128,768]{1,0:T(8,128)} %copy-done.8) | copy-start | bytes 1179652
  205.0 13.8 %copy-start.11 = (f32[128,768]{1,0:T(8,128)S(1)}, f32[128,768]{1,0:T(8,128)}, u32[]{:S(2)}) copy-start(f32[128,768]{1,0:T(8,128)} %copy-done.10) | copy-start | bytes 1179652
  (10 other events, 32.7 us)
Sparse Core Ops, SparseCore 0:
  10.1 92.6 all-gather.4
  104.8 75.8 all-gather.2
  184.1 75.8 reduce-scatter.1
